TPU v7x, 128 devices: a whole 4x4x4 slice. The times are simulated.
128 devices in a mesh: rad: 4 (over x_hi, core), sec: 32 (over x_lo, y, z).
Axes of the slice: x: 4 (x_hi: 2, x_lo: 2; x = x_hi * 2 + x_lo), y: 4, z: 4, core: 2. Of those that a mesh axis runs over, the one named last changes fastest.
Arguments:
- gas_fields: float32 [5, 128, 16, 8192], P(None, 'rad', None, 'sec'), may hold values from -8 to 8, as said below
- orbit_shift: int32 [128], P('rad'), may hold values from 0 to 8191
- particle_velocity: float32 [3, 524288], P(None, ('rad', 'sec')), may hold values from -6 to 6
- particle_mass: float32 [524288], P(('rad', 'sec')), may hold values from 0.2 to 2
- particle_stop: float32 [524288], P(('rad', 'sec')), may hold values from 0.1 to 10
- particle_cell: int32 [524288], P(('rad', 'sec')), may hold values from 0 to 131071
- particle_dest: int32 [524288, 1], P(('rad', 'sec')), may hold values from 0 to 127; in each aligned block of 4096 rows (0 to 4095, 4096 to 8191, ...) at most 64 rows name the same one
Outputs:
- gas_next: float32 [5, 128, 16, 8192], P(None, 'rad', None, 'sec')
- arrived_velocity: float32 [3, 1048576], P(None, ('rad', 'sec'))
Inputs may be any that keep to these rules, and one draw needn't show every extreme that they name: `gas_fields`: field 0 (density) lies between 0.25 and 4 and momentum over density between -2 and 2. `particle_dest`: among the 4096 particles of one device at most 64 name the same destination; in every draw some device sends exactly 64 to one destination.
All inputs are finite; a program needn't handle non-finite values.
Results may differ from a plain program's by a relative error of at most 0.0003.
Values sent between devices are 32-bit elements; how exact they have to be, the bound alone decides.
No kernel may reach another device: no remote copies, remote signals or barrier semaphores. Data moves between devices by JAX's collectives and lax.ppermute only.
A program may use at most 128 MiB of HBM per device.

v0:
```python
import jax
import jax.numpy as jnp
from jax import lax
from jax.sharding import PartitionSpec as P

sound_speed = 1.0
radial_rate = 0.2
azimuth_rate = 0.2
exact = lax.Precision.HIGHEST


def passed_along(block, axis, distance):
    devices = range(lax.axis_size(axis))
    route = [((i - distance) % len(devices), i) for i in devices]
    return lax.ppermute(block, axis, route)


def with_halo(cells, sides, width, closed):
    for axis, dim in sides:
        count = lax.axis_size(axis)
        ends = count if closed else count - 1
        head = lax.slice_in_dim(cells, 0, width, axis=dim)
        tail = lax.slice_in_dim(cells, cells.shape[dim] - width, cells.shape[dim], axis=dim)
        cells = jnp.concatenate(
            [
                lax.ppermute(tail, axis, [(i, (i + 1) % count) for i in range(ends)]),
                cells,
                lax.ppermute(head, axis, [((i + 1) % count, i) for i in range(ends)]),
            ],
            axis=dim,
        )
    return cells


def limited_slope(left_step, right_step):
    return (
        0.5
        * (jnp.sign(left_step) + jnp.sign(right_step))
        * jnp.minimum(jnp.abs(left_step), jnp.abs(right_step))
    )


def plm_divergence(values, speed, along_axis, extent):

    def take_range(source, offset_at, length):
        return lax.slice_in_dim(source, offset_at, offset_at + length, axis=along_axis)

    left_step = take_range(values, 1, extent + 2) - take_range(values, 0, extent + 2)
    right_step = take_range(values, 2, extent + 2) - take_range(values, 1, extent + 2)
    slopes = limited_slope(left_step, right_step)
    centre = take_range(values, 1, extent + 2)
    left_value = take_range(centre, 0, extent + 1) + 0.5 * take_range(slopes, 0, extent + 1)
    right_value = take_range(centre, 1, extent + 1) - 0.5 * take_range(slopes, 1, extent + 1)
    face_speed = 0.5 * (take_range(speed, 1, extent + 1) + take_range(speed, 2, extent + 1))
    face_flux = face_speed * 0.5 * (left_value + right_value) - 0.5 * (
        jnp.abs(face_speed) + sound_speed
    ) * (right_value - left_value)
    return take_range(face_flux, 1, extent) - take_range(face_flux, 0, extent)


def local(
    gas_fields,
    orbit_shift,
    particle_velocity,
    particle_mass,
    particle_stop,
    particle_cell,
    particle_dest,
):
    field_count, radius_count, layers, sector = gas_fields.shape
    sectors = lax.axis_size("sec")
    quotient = orbit_shift // sector
    remainder = orbit_shift % sector
    carried = gas_fields
    for bit_level in range(sectors.bit_length() - 1):
        incoming = passed_along(carried, "sec", 1 << bit_level)
        chosen = quotient >> bit_level & 1 == 1
        carried = jnp.where(chosen[None, :, None, None], incoming, carried)
    preceding = passed_along(carried, "sec", 1)
    window = jnp.concatenate([preceding, carried], axis=3)
    for bit_level in range((sector - 1).bit_length()):
        step_size = 1 << bit_level
        moved = jnp.concatenate(
            [
                jnp.zeros((field_count, radius_count, layers, step_size), jnp.float32),
                window[..., :-step_size],
            ],
            axis=3,
        )
        chosen = remainder >> bit_level & 1 == 1
        window = jnp.where(chosen[None, :, None, None], moved, window)
    shifted = window[..., sector:]
    per_device = particle_dest.shape[0]
    devices = lax.axis_size(("rad", "sec"))
    capacity = 2 * per_device // devices
    target = particle_dest[:, 0]
    hits = target[:, None] == jnp.arange(devices, dtype=jnp.int32)[None, :]
    order_index = jnp.arange(per_device, dtype=jnp.int32)
    earlier = (order_index[:, None] >= order_index[None, :]).astype(jnp.bfloat16)
    running = jnp.dot(earlier, hits.astype(jnp.bfloat16), preferred_element_type=jnp.float32)
    slot = jnp.sum(jnp.where(hits, running, 0.0), axis=1).astype(jnp.int32) - 1
    column = target * capacity + slot
    records = jnp.concatenate(
        [
            particle_velocity,
            particle_mass[None],
            particle_stop[None],
            particle_cell[None].astype(jnp.float32),
        ],
        axis=0,
    )
    block_rows = min(512, per_device)
    block_count = per_device // block_rows
    record_blocks = records.reshape(6, block_count, block_rows).transpose(1, 0, 2)
    column_blocks = column.reshape(block_count, block_rows)
    slot_ids = jnp.arange(devices * capacity, dtype=jnp.int32)

    def place_block(total, pair):
        record_block, column_block = pair
        placing = (column_block[:, None] == slot_ids[None, :]).astype(jnp.float32)
        return (
            total
            + jnp.dot(record_block, placing, precision=exact, preferred_element_type=jnp.float32),
            None,
        )

    outbox_flat, _ = lax.scan(
        place_block, jnp.zeros((6, devices * capacity), jnp.float32), (record_blocks, column_blocks)
    )
    outbox = outbox_flat.reshape(6, devices, capacity)
    inbox = lax.all_to_all(outbox, ("rad", "sec"), split_axis=1, concat_axis=1, tiled=True)
    received = inbox.reshape(6, devices * capacity)
    row_count = radius_count * layers
    velocity_rows = (
        (shifted[1:4] / shifted[0:1])
        .reshape(3, row_count, sector)
        .transpose(1, 0, 2)
        .reshape(row_count, 3 * sector)
    )
    cells = received[5].astype(jnp.int32)
    row_hot = (
        (cells // sector)[:, None] == jnp.arange(row_count, dtype=jnp.int32)[None, :]
    ).astype(jnp.float32)
    azimuth_hot = (
        (cells % sector)[:, None] == jnp.arange(sector, dtype=jnp.int32)[None, :]
    ).astype(jnp.float32)
    picked = jnp.dot(
        row_hot, velocity_rows, precision=exact, preferred_element_type=jnp.float32
    ).reshape(-1, 3, sector)
    local_speed = jnp.sum(picked * azimuth_hot[:, None, :], axis=2).T
    velocity_in = received[0:3]
    fraction = received[4] / (1.0 + received[4])
    change = (velocity_in - local_speed) * fraction[None]
    arrived_velocity = velocity_in - change
    impulse = received[3][None] * change
    spread = (impulse.T[:, :, None] * azimuth_hot[:, None, :]).reshape(-1, 3 * sector)
    deposit_rows = jnp.dot(row_hot.T, spread, precision=exact, preferred_element_type=jnp.float32)
    momentum_added = (
        deposit_rows.reshape(row_count, 3, sector)
        .transpose(1, 0, 2)
        .reshape(3, radius_count, layers, sector)
    )
    dragged = jnp.concatenate([shifted[0:1], shifted[1:4] + momentum_added, shifted[4:5]], axis=0)
    radial_speed = dragged[1] / dragged[0]
    azimuthal_speed = dragged[2] / dragged[0]
    stacked = jnp.concatenate([dragged, radial_speed[None], azimuthal_speed[None]], axis=0)
    radial_pad = with_halo(stacked, (("rad", 1),), 2, False)
    azimuth_pad = with_halo(stacked, (("sec", 3),), 2, True)
    radial_change = plm_divergence(radial_pad[0:5], radial_pad[5:6], 1, radius_count)
    azimuth_change = plm_divergence(azimuth_pad[0:5], azimuth_pad[6:7], 3, sector)
    gas_next = dragged - radial_rate * radial_change - azimuth_rate * azimuth_change
    return (gas_next, arrived_velocity)


def solution(mesh):
    placed = (
        P(None, "rad", None, "sec"),
        P("rad"),
        P(None, ("rad", "sec")),
        P(("rad", "sec")),
        P(("rad", "sec")),
        P(("rad", "sec")),
        P(("rad", "sec"), None),
    )
    return jax.shard_map(
        local,
        mesh=mesh,
        in_specs=placed,
        out_specs=(P(None, "rad", None, "sec"), P(None, ("rad", "sec"))),
        check_vma=False,
    )
```

profile of v0, /device:TPU:1, one launch (start us, length us, event | category | flops | bytes accessed | tf_op | source)
XLA Modules:
  0.0 500.7 jit_solution(4476107903149512825)
XLA Ops:
  4.4 61.0 %collective-permute-done = f32[5,32,16,256]{3,2,1,0:T(8,128)S(1)} collective-permute-done((f32[5,32,16,256]{3,2,1,0:T(8,128)}, f32[5,32,16,256]{3,2,1,0:T(8,128)S(1)}, u32[]{:S(2)}, u32[]{:S(2)}) %collective-permute-start) | collective-permute-done | bytes 2621472 | tf_op jit(solution)/shard_map/ppermute | solution.py:15
  67.7 61.7 %collective-permute-done.1 = f32[5,32,16,256]{3,2,1,0:T(8,128)S(1)} collective-permute-done((f32[5,32,16,256]{3,2,1,0:T(8,128)S(1)}, f32[5,32,16,256]{3,2,1,0:T(8,128)S(1)}, u32[]{:S(2)}, u32[]{:S(2)}) %collective-permute-start.1) | collective-permute-done | bytes 2621472 | tf_op jit(solution)/shard_map/ppermute | solution.py:15
  129.7 58.4 %collective-permute-done.2 = f32[5,32,16,256]{3,2,1,0:T(8,128)S(1)} collective-permute-done((f32[5,32,16,256]{3,2,1,0:T(8,128)S(1)}, f32[5,32,16,256]{3,2,1,0:T(8,128)S(1)}, u32[]{:S(2)}, u32[]{:S(2)}) %collective-permute-start.2) | collective-permute-done | bytes 2621472 | tf_op jit(solution)/shard_map/ppermute | solution.py:15
  189.0 19.8 %fusion.41 = f32[4096]{0:T(1024)S(1)} fusion(s32[4096]{0:T(1024)S(1)} %bitcast.89), kind=kOutput, calls=%fused_computation.88 | convolution fusion | flops 4313837568 | bytes 32768 | tf_op jit(solution)/shard_map/dot_general | solution.py:100
  209.0 37.6 %collective-permute-done.3 = f32[5,32,16,256]{3,2,1,0:T(8,128)} collective-permute-done((f32[5,32,16,256]{3,2,1,0:T(8,128)S(1)}, f32[5,32,16,256]{3,2,1,0:T(8,128)}, u32[]{:S(2)}, u32[]{:S(2)}) %collective-permute-start.3) | collective-permute-done | bytes 2621472 | tf_op jit(solution)/shard_map/ppermute | solution.py:15
  246.5 2.8 broadcast_select_fusion.3
  250.9 43.1 %while.11 = (s32[]{:T(128)}, f32[6,8192]{1,0:T(8,128)S(1)}, f32[8,6,512]{2,1,0:T(8,128)S(1)}, s32[8,512]{1,0:T(8,128)S(1)}, s32[]{:T(128)}, /*index=5*/s32[]{:T(128)}) while((s32[]{:T(128)}, f32[6,8192]{1,0:T(8,128)S(1)}, f32[8,6,512]{2,1,0:T(8,128)S(1)}, s32[8,512]{1,0:T(8,128)S(1)}, s32[]{:T(128)}, /*index=5*/s32[]{:T(128)}) %tuple.50), condition=%wide.region_2.3_spmd.clone, body=%wide.region_1.2_spmd.clone.sunk | while | flops 306282496 | bytes 481375 | solution.py:127
  250.9 5.4 %fusion.60 = f32[6,8192]{1,0:T(8,128)S(1)} fusion(s32[512]{0:T(512)S(1)} %bitcast.88, f32[6,8192]{1,0:T(8,128)S(1)} %get-tuple-element.124, pred[]{:T(512)S(6)} %compare.25, f32[8,6,512]{2,1,0:T(8,128)S(1)} %get-tuple-element.131, s32[]{:T(128)S(6)} %copy.30), kind=kOutput, calls=%fused_computation.3.clone.1 | convolution fusion | flops 306282496 | bytes 477189 | tf_op jit(solution)/shard_map/while/body/eval_jaxpr/dot_general | solution.py:123
  256.3 5.4 %fusion.60 = f32[6,8192]{1,0:T(8,128)S(1)} fusion(s32[512]{0:T(512)S(1)} %bitcast.88, f32[6,8192]{1,0:T(8,128)S(1)} %get-tuple-element.124, pred[]{:T(512)S(6)} %compare.25, f32[8,6,512]{2,1,0:T(8,128)S(1)} %get-tuple-element.131, s32[]{:T(128)S(6)} %copy.30), kind=kOutput, calls=%fused_computation.3.clone.1 | convolution fusion | flops 306282496 | bytes 477189 | tf_op jit(solution)/shard_map/while/body/eval_jaxpr/dot_general | solution.py:123
  261.7 5.4 %fusion.60 = f32[6,8192]{1,0:T(8,128)S(1)} fusion(s32[512]{0:T(512)S(1)} %bitcast.88, f32[6,8192]{1,0:T(8,128)S(1)} %get-tuple-element.124, pred[]{:T(512)S(6)} %compare.25, f32[8,6,512]{2,1,0:T(8,128)S(1)} %get-tuple-element.131, s32[]{:T(128)S(6)} %copy.30), kind=kOutput, calls=%fused_computation.3.clone.1 | convolution fusion | flops 306282496 | bytes 477189 | tf_op jit(solution)/shard_map/while/body/eval_jaxpr/dot_general | solution.py:123
  267.1 5.4 %fusion.60 = f32[6,8192]{1,0:T(8,128)S(1)} fusion(s32[512]{0:T(512)S(1)} %bitcast.88, f32[6,8192]{1,0:T(8,128)S(1)} %get-tuple-element.124, pred[]{:T(512)S(6)} %compare.25, f32[8,6,512]{2,1,0:T(8,128)S(1)} %get-tuple-element.131, s32[]{:T(128)S(6)} %copy.30), kind=kOutput, calls=%fused_computation.3.clone.1 | convolution fusion | flops 306282496 | bytes 477189 | tf_op jit(solution)/shard_map/while/body/eval_jaxpr/dot_general | solution.py:123
  272.5 5.4 %fusion.60 = f32[6,8192]{1,0:T(8,128)S(1)} fusion(s32[512]{0:T(512)S(1)} %bitcast.88, f32[6,8192]{1,0:T(8,128)S(1)} %get-tuple-element.124, pred[]{:T(512)S(6)} %compare.25, f32[8,6,512]{2,1,0:T(8,128)S(1)} %get-tuple-element.131, s32[]{:T(128)S(6)} %copy.30), kind=kOutput, calls=%fused_computation.3.clone.1 | convolution fusion | flops 306282496 | bytes 477189 | tf_op jit(solution)/shard_map/while/body/eval_jaxpr/dot_general | solution.py:123
  277.9 5.4 %fusion.60 = f32[6,8192]{1,0:T(8,128)S(1)} fusion(s32[512]{0:T(512)S(1)} %bitcast.88, f32[6,8192]{1,0:T(8,128)S(1)} %get-tuple-element.124, pred[]{:T(512)S(6)} %compare.25, f32[8,6,512]{2,1,0:T(8,128)S(1)} %get-tuple-element.131, s32[]{:T(128)S(6)} %copy.30), kind=kOutput, calls=%fused_computation.3.clone.1 | convolution fusion | flops 306282496 | bytes 477189 | tf_op jit(solution)/shard_map/while/body/eval_jaxpr/dot_general | solution.py:123
  283.3 5.4 %fusion.60 = f32[6,8192]{1,0:T(8,128)S(1)} fusion(s32[512]{0:T(512)S(1)} %bitcast.88, f32[6,8192]{1,0:T(8,128)S(1)} %get-tuple-element.124, pred[]{:T(512)S(6)} %compare.25, f32[8,6,512]{2,1,0:T(8,128)S(1)} %get-tuple-element.131, s32[]{:T(128)S(6)} %copy.30), kind=kOutput, calls=%fused_computation.3.clone.1 | convolution fusion | flops 306282496 | bytes 477189 | tf_op jit(solution)/shard_map/while/body/eval_jaxpr/dot_general | solution.py:123
  288.7 5.4 %fusion.60 = f32[6,8192]{1,0:T(8,128)S(1)} fusion(s32[512]{0:T(512)S(1)} %bitcast.88, f32[6,8192]{1,0:T(8,128)S(1)} %get-tuple-element.124, pred[]{:T(512)S(6)} %compare.25, f32[8,6,512]{2,1,0:T(8,128)S(1)} %get-tuple-element.131, s32[]{:T(128)S(6)} %copy.30), kind=kOutput, calls=%fused_computation.3.clone.1 | convolution fusion | flops 306282496 | bytes 477189 | tf_op jit(solution)/shard_map/while/body/eval_jaxpr/dot_general | solution.py:123
  295.4 7.4 %all-to-all-start = ((f32[128,1,384]{2,1,0:T(1,128)}), f32[128,1,384]{2,1,0:T(1,128)S(1)}, u32[]{:S(2)}, u32[]{:S(2)}) async-start(f32[128,1,384]{2,1,0:T(1,128)} %reshape.158), calls=%async_computation | async-start | bytes 393216 | tf_op jit(solution)/shard_map/all_to_all | solution.py:131
  304.1 8.9 %all-to-all-done = f32[128,1,384]{2,1,0:T(1,128)S(1)} async-done(((f32[128,1,384]{2,1,0:T(1,128)}), f32[128,1,384]{2,1,0:T(1,128)S(1)}, u32[]{:S(2)}, u32[]{:S(2)}) %all-to-all-start) | async-done | bytes 196640 | tf_op jit(solution)/shard_map/all_to_all | solution.py:131
  314.8 2.9 broadcast_select_fusion.4
  319.6 4.2 fusion.20
  323.8 55.8 %collective-permute-done.5 = f32[5,32,16,256]{3,2,1,0:T(8,128)} collective-permute-done((f32[5,32,16,256]{3,2,1,0:T(8,128)S(1)}, f32[5,32,16,256]{3,2,1,0:T(8,128)}, u32[]{:S(2)}, u32[]{:S(2)}) %collective-permute-start.5) | collective-permute-done | bytes 2621472 | tf_op jit(solution)/shard_map/ppermute | solution.py:15
  382.0 3.3 fusion.22
  401.3 22.5 %multiply_reduce_fusion = f32[8192,3]{0,1:T(4,128)S(1)} fusion(f32[8192,256]{0,1:T(8,128)} %fusion.20, f32[512,3,256]{0,2,1:T(8,128)S(1)} %copy.16, s32[8192]{0:T(1024)S(1)} %get-tuple-element.77), kind=kOutput, calls=%fused_computation.14 | convolution fusion | flops 38671458304 | bytes 10092544 | tf_op jit(solution)/shard_map/dot_general | solution.py:147
  424.6 25.1 %fusion.9 = f32[512,3,256]{2,0,1:T(8,128)S(1)} fusion(f32[8192,3]{0,1:T(4,128)S(1)} %get-tuple-element.76, f32[8192,256]{0,1:T(8,128)} %fusion.20, s32[8192]{0:T(1024)S(1)} %get-tuple-element.77), kind=kOutput, calls=%fused_computation.11 | convolution fusion | flops 38665191424 | bytes 10092544 | tf_op jit(solution)/shard_map/dot_general | solution.py:157
  449.7 2.9 constant_dynamic-update-slice_fusion.1
  458.3 3.9 fusion.56
  469.4 4.4 collective-permute-start.7
  473.8 3.1 collective-permute-start.6
  478.6 2.9 copy.19
  481.5 6.8 %minimum_multiply_fusion = f32[5,32,16,258]{3,2,1,0:T(8,128)S(1)} fusion(f32[7,32,16,2]{3,2,1,0:T(8,128)S(1)} %copy.21, f32[7,32,16,256]{3,2,1,0:T(8,128)} %fusion.47, f32[7,32,16,2]{3,2,1,0:T(8,128)} %copy.19), kind=kLoop, calls=%fused_computation.54 | loop fusion | flops 9246720 | bytes 6369280 | tf_op jit(solution)/shard_map/mul | solution.py:37
  488.8 2.7 multiply_subtract_fusion
  492.5 3.0 minimum_multiply_fusion.1
  498.0 2.5 fusion.37
  (108 shorter events, 52.6 us)
Async XLA Ops:
  0.6 64.8 %collective-permute-start = (f32[5,32,16,256]{3,2,1,0:T(8,128)}, f32[5,32,16,256]{3,2,1,0:T(8,128)S(1)}, u32[]{:S(2)}, u32[]{:S(2)}) collective-permute-start(f32[5,32,16,256]{3,2,1,0:T(8,128)} %param.9), channel_id=1, source_target_pairs={{31,0},{0,1},{1,2},{2,3},{3,4},{4,5},{5,6},{6,7},{7,8},{8,9},{9,10... | collective-permute-start | bytes 7864328 | tf_op jit(solution)/shard_map/ppermute | solution.py:15
  67.6 61.8 %collective-permute-start.1 = (f32[5,32,16,256]{3,2,1,0:T(8,128)S(1)}, f32[5,32,16,256]{3,2,1,0:T(8,128)S(1)}, u32[]{:S(2)}, u32[]{:S(2)}) collective-permute-start(f32[5,32,16,256]{3,2,1,0:T(8,128)S(1)} %broadcast_select_fusion), channel_id=1, source_target_pairs={{30,0},{31,1},{0,2},{1,3},{2,4},{3,5},{4,6},{5,7},{6,8},{7,9},{8,1... | collective-permute-start | bytes 7864328 | tf_op jit(solution)/shard_map/ppermute | solution.py:15
  129.7 58.5 %collective-permute-start.2 = (f32[5,32,16,256]{3,2,1,0:T(8,128)S(1)}, f32[5,32,16,256]{3,2,1,0:T(8,128)S(1)}, u32[]{:S(2)}, u32[]{:S(2)}) collective-permute-start(f32[5,32,16,256]{3,2,1,0:T(8,128)S(1)} %broadcast_select_fusion.1), channel_id=1, source_target_pairs={{28,0},{29,1},{30,2},{31,3},{0,4},{1,5},{2,6},{3,7},{4,8},{5,9},{6... | collective-permute-start | bytes 7864328 | tf_op jit(solution)/shard_map/ppermute | solution.py:15
  188.2 0.7 copy-start.8
  188.2 0.7 copy-start.9
  188.5 20.3 %copy-start.4 = (f32[5,32,16,256]{3,2,1,0:T(8,128)}, f32[5,32,16,256]{3,2,1,0:T(8,128)S(1)}, u32[]{:S(2)}) copy-start(f32[5,32,16,256]{3,2,1,0:T(8,128)S(1)} %broadcast_select_fusion.2) | copy-start | bytes 7864324
  188.5 58.0 %collective-permute-start.3 = (f32[5,32,16,256]{3,2,1,0:T(8,128)S(1)}, f32[5,32,16,256]{3,2,1,0:T(8,128)}, u32[]{:S(2)}, u32[]{:S(2)}) collective-permute-start(f32[5,32,16,256]{3,2,1,0:T(8,128)S(1)} %broadcast_select_fusion.2), channel_id=1, source_target_pairs={{24,0},{25,1},{26,2},{27,3},{28,4},{29,5},{30,6},{31,7},{0,8},{1,9... | collective-permute-start | bytes 7864328 | tf_op jit(solution)/shard_map/ppermute | solution.py:15
  188.9 19.9 %copy-start.7 = (f32[3,4096]{1,0:T(4,128)S(1)}, f32[3,4096]{1,0:T(4,128)}, u32[]{:S(2)}) copy-start(f32[3,4096]{1,0:T(4,128)} %param.11) | copy-start | bytes 147460
  189.0 19.9 %copy-start.10 = (f32[4096]{0:T(1024)S(1)}, f32[4096]{0:T(1024)}, u32[]{:S(2)}) copy-start(f32[4096]{0:T(1024)} %param.13) | copy-start | bytes 49156
  189.0 19.9 %copy-start.11 = (f32[4096]{0:T(1024)S(1)}, f32[4096]{0:T(1024)}, u32[]{:S(2)}) copy-start(f32[4096]{0:T(1024)} %param.12) | copy-start | bytes 49156
  249.4 1.5 copy-start.3
  249.4 65.4 %collective-permute-start.4 = (f32[5,32,16,256]{3,2,1,0:T(8,128)S(1)}, f32[5,32,16,256]{3,2,1,0:T(8,128)}, u32[]{:S(2)}, u32[]{:S(2)}) collective-permute-start(f32[5,32,16,256]{3,2,1,0:T(8,128)S(1)} %broadcast_select_fusion.3), channel_id=1, source_target_pairs={{16,0},{17,1},{18,2},{19,3},{20,4},{21,5},{22,6},{23,7},{24,8},{25... | collective-permute-start | bytes 7864328 | tf_op jit(solution)/shard_map/ppermute | solution.py:15
  295.4 17.6 %all-to-all-start = ((f32[128,1,384]{2,1,0:T(1,128)}), f32[128,1,384]{2,1,0:T(1,128)S(1)}, u32[]{:S(2)}, u32[]{:S(2)}) async-start(f32[128,1,384]{2,1,0:T(1,128)} %reshape.158), calls=%async_computation | async-start | bytes 393216 | tf_op jit(solution)/shard_map/all_to_all | solution.py:131
  317.6 61.9 %collective-permute-start.5 = (f32[5,32,16,256]{3,2,1,0:T(8,128)S(1)}, f32[5,32,16,256]{3,2,1,0:T(8,128)}, u32[]{:S(2)}, u32[]{:S(2)}) collective-permute-start(f32[5,32,16,256]{3,2,1,0:T(8,128)S(1)} %broadcast_select_fusion.4), channel_id=1, source_target_pairs={{31,0},{0,1},{1,2},{2,3},{3,4},{4,5},{5,6},{6,7},{7,8},{8,9},{9,10... | collective-permute-start | bytes 7864328 | tf_op jit(solution)/shard_map/ppermute | solution.py:15
  323.8 58.1 %copy-start.14 = (pred[32]{0:T(512)(128)(4,1)S(1)}, pred[32]{0:T(512)(128)(4,1)}, u32[]{:S(2)}) copy-start(pred[32]{0:T(512)(128)(4,1)} %get-tuple-element.85) | copy-start | bytes 100
  381.9 3.3 copy-start.13
  385.3 1.8 copy-start.12
  396.0 0.7 copy-start.15
  397.6 2.9 copy-start.2
  464.5 12.3 %collective-permute-start.9 = (f32[7,32,16,2]{1,2,3,0:T(8,128)S(1)}, f32[7,32,16,2]{1,2,3,0:T(8,128)}, u32[]{:S(2)}, u32[]{:S(2)}) collective-permute-start(f32[7,32,16,2]{1,2,3,0:T(8,128)S(1)} %copy.20), channel_id=1, source_target_pairs={{1,0},{2,1},{3,2},{4,3},{5,4},{6,5},{7,6},{8,7},{9,8},{10,9},{11,1... | collective-permute-start | bytes 86024 | tf_op jit(solution)/shard_map/ppermute | solution.py:28
  466.0 12.5 %collective-permute-start.8 = (f32[7,32,16,2]{1,2,3,0:T(8,128)}, f32[7,32,16,2]{1,2,3,0:T(8,128)}, u32[]{:S(2)}, u32[]{:S(2)}) collective-permute-start(f32[7,32,16,2]{1,2,3,0:T(8,128)} %copy.18), channel_id=1, source_target_pairs={{0,1},{1,2},{2,3},{3,4},{4,5},{5,6},{6,7},{7,8},{8,9},{9,10},{10,1... | collective-permute-start | bytes 86024 | tf_op jit(solution)/shard_map/ppermute | solution.py:26
  469.4 22.1 %collective-permute-start.7 = (f32[7,2,16,256]{3,2,1,0:T(8,128)}, f32[7,2,16,256]{3,2,1,0:T(8,128)}, u32[]{:S(2)}, u32[]{:S(2)}) collective-permute-start(f32[7,2,16,256]{3,2,1,0:T(8,128)} %get-tuple-element.72), channel_id=1, source_target_pairs={{32,0},{64,32},{96,64},{33,1},{65,33},{97,65},{34,2},{66,34},{98,6... | collective-permute-start | bytes 688136 | tf_op jit(solution)/shard_map/ppermute | solution.py:28
  473.8 17.7 %collective-permute-start.6 = (f32[7,2,16,256]{3,2,1,0:T(8,128)}, f32[7,2,16,256]{3,2,1,0:T(8,128)}, u32[]{:S(2)}, u32[]{:S(2)}) collective-permute-start(f32[7,2,16,256]{3,2,1,0:T(8,128)} %get-tuple-element.71), channel_id=1, source_target_pairs={{0,32},{32,64},{64,96},{1,33},{33,65},{65,97},{2,34},{34,66},{66,9... | collective-permute-start | bytes 688136 | tf_op jit(solution)/shard_map/ppermute | solution.py:26
  481.5 6.8 %copy-start = (f32[7,32,16,256]{3,2,1,0:T(8,128)S(1)}, f32[7,32,16,256]{3,2,1,0:T(8,128)}, u32[]{:S(2)}) copy-start(f32[7,32,16,256]{3,2,1,0:T(8,128)} %fusion.47) | copy-start | bytes 11010052
  481.5 6.8 %copy-start.1 = (f32[7,32,16,2]{3,2,1,0:T(8,128)S(1)}, f32[7,32,16,2]{3,2,1,0:T(8,128)}, u32[]{:S(2)}) copy-start(f32[7,32,16,2]{3,2,1,0:T(8,128)} %copy.19) | copy-start | bytes 86020
  495.5 2.5 copy-start.5
  495.5 2.5 copy-start.6
where the time goes:
time: 506 us; the launch traced here: 501 us
  waiting for transfers between devices  283 us (56%)
  matrix products  110 us (22%)
  other arithmetic  60.7 us (12%)
  local copies, waits for them, and re-layouts  24.2 us (5%)
  starting transfers between devices  20.4 us (4%)
    ppermute x6, waiting for transfers between devices, passed_along(): return lax.ppermute(block, axis, route)  274 us
    dot_general x8, matrix products, place_block(): jnp.dot(record_block, placing, precision=exact, preferred_element_type=jn...  43 us
    dot_general x1, matrix products, local(): jnp.dot(row_hot.T, spread, precision=exact, preferred_element_type=jnp.fl...  25.1 us
    dot_general x1, matrix products, local(): jnp.dot(row_hot, velocity_rows, precision=exact, preferred_element_type=j...  22.5 us
    dot_general x1, matrix products, local(): jnp.dot(earlier, hits.astype(jnp.bfloat16), preferred_element_type=jnp.fl...  19.8 us
    select_n x8, other arithmetic, local(): window = jnp.where(chosen[None, :, None, None], moved, window)  14.9 us
  transfers between devices with their start and end apart: 11, of which 6 were waited for; matrix products, arithmetic and copies ran while one was open for 18% of the time, Pallas kernels for 0%

commit v1 on v0

--- a/solution.py
+++ b/solution.py
@@ -69,27 +69,22 @@
 ):
     field_count, radius_count, layers, sector = gas_fields.shape
     sectors = lax.axis_size("sec")
-    quotient = orbit_shift // sector
-    remainder = orbit_shift % sector
-    carried = gas_fields
-    for bit_level in range(sectors.bit_length() - 1):
-        incoming = passed_along(carried, "sec", 1 << bit_level)
-        chosen = quotient >> bit_level & 1 == 1
-        carried = jnp.where(chosen[None, :, None, None], incoming, carried)
-    preceding = passed_along(carried, "sec", 1)
-    window = jnp.concatenate([preceding, carried], axis=3)
-    for bit_level in range((sector - 1).bit_length()):
-        step_size = 1 << bit_level
-        moved = jnp.concatenate(
-            [
-                jnp.zeros((field_count, radius_count, layers, step_size), jnp.float32),
-                window[..., :-step_size],
-            ],
-            axis=3,
-        )
-        chosen = remainder >> bit_level & 1 == 1
-        window = jnp.where(chosen[None, :, None, None], moved, window)
-    shifted = window[..., sector:]
+    per_member = radius_count // sectors
+    member = lax.axis_index("sec")
+    ring = lax.all_to_all(gas_fields, "sec", split_axis=1, concat_axis=3, tiled=True)
+    extent = ring.shape[3]
+    own_shift = lax.dynamic_slice_in_dim(orbit_shift, member * per_member, per_member)
+    doubled = jnp.concatenate([ring, ring], axis=3)
+    rolled = jnp.concatenate(
+        [
+            lax.dynamic_slice_in_dim(
+                doubled[:, i : i + 1], (extent - own_shift[i]) % extent, extent, axis=3
+            )
+            for i in range(per_member)
+        ],
+        axis=1,
+    )
+    shifted = lax.all_to_all(rolled, "sec", split_axis=3, concat_axis=1, tiled=True)
     per_device = particle_dest.shape[0]
     devices = lax.axis_size(("rad", "sec"))
     capacity = 2 * per_device // devices

time: 506 us -> 524 us (1.036)
  waiting for transfers between devices: 283 us -> 66.8 us
  local copies, waits for them, and re-layouts: 24.2 us -> 180 us
  other arithmetic: 60.7 us -> 107 us
  starting transfers between devices: 20.4 us -> 35.9 us
  matrix products: 110 us -> 121 us
    ppermute x6 -> x0, waiting for transfers between devices: 274 us -> none  [passed_along(): return lax.ppermute(block, axis, route)]
    unnamed x35 -> x30, local copies, waits for them, and re-layouts: 5.74 us -> 88.4 us
    unnamed x3 -> x4, other arithmetic: 4.86 us -> 71.1 us
    all_to_all x0 -> x2, waiting for transfers between devices: none -> 58.4 us  [the longest x1 30.3 us: local(): lax.all_to_all(gas_fields, 'sec', split_axis=1, concat_axis=3, tiled=True)]
    all_to_all x1 -> x2, local copies, waits for them, and re-layouts: 0.54 us -> 38.7 us  [the longest x1 38.4 us: local(): lax.all_to_all(rolled, 'sec', split_axis=3, concat_axis=1, tiled=True)]
    dynamic_slice x0 -> x2, local copies, waits for them, and re-layouts: none -> 29.8 us  [the longest x1 29.2 us: local(): lax.dynamic_slice_in_dim(doubled[:, i:i + 1], (extent - own_shift[i]) % e...]
    select_n x13 -> x0, other arithmetic: 23.4 us -> none  [the longest x8 14.9 us: local(): window = jnp.where(chosen[None, :, None, None], moved, window)]
    all_to_all x0 -> x2, starting transfers between devices: none -> 10.8 us  [the longest x1 6.51 us: local(): lax.all_to_all(rolled, 'sec', split_axis=3, concat_axis=1, tiled=True)]
  transfers between devices with their start and end apart: 11 -> 7, of which waited for: 6 -> 3; matrix products, arithmetic and copies ran while one was open for 18% -> 5% of each run, Pallas kernels for 0% -> 0%
where the time goes in v1:
time: 524 us; the launch traced here: 514 us
  local copies, waits for them, and re-layouts  180 us (34%)
  matrix products  121 us (23%)
  other arithmetic  107 us (20%)
  waiting for transfers between devices  66.8 us (13%)
  starting transfers between devices  35.9 us (7%)
    unnamed x30, local copies, waits for them, and re-layouts  88.4 us
    unnamed x4, other arithmetic  71.1 us
    dot_general x8, matrix products, place_block(): jnp.dot(record_block, placing, precision=exact, preferred_element_type=jn...  43 us
    all_to_all x1, local copies, waits for them, and re-layouts, local(): lax.all_to_all(rolled, 'sec', split_axis=3, concat_axis=1, tiled=True)  38.4 us
    dot_general x1, matrix products, local(): jnp.dot(row_hot, velocity_rows, precision=exact, preferred_element_type=j...  31 us
    all_to_all x1, waiting for transfers between devices, local(): lax.all_to_all(gas_fields, 'sec', split_axis=1, concat_axis=3, tiled=True)  30.3 us
    dynamic_slice x1, local copies, waits for them, and re-layouts, local(): lax.dynamic_slice_in_dim(doubled[:, i:i + 1], (extent - own_shift[i]) % e...  29.2 us
    all_to_all x1, waiting for transfers between devices, local(): lax.all_to_all(rolled, 'sec', split_axis=3, concat_axis=1, tiled=True)  28.1 us
  transfers between devices with their start and end apart: 7, of which 3 were waited for; matrix products, arithmetic and copies ran while one was open for 5% of the time, Pallas kernels for 0%

profile of v1, /device:TPU:1, one launch (start us, length us, event | category | flops | bytes accessed | tf_op | source)
XLA Modules:
  0.0 513.9 jit_solution(7381973923814535603)
XLA Ops:
  2.2 20.6 %fusion.40 = f32[4096]{0:T(1024)S(1)} fusion(s32[4096]{0:T(1024)} %bitcast.122), kind=kOutput, calls=%fused_computation.74 | convolution fusion | flops 4313837568 | bytes 32768 | tf_op jit(solution)/shard_map/dot_general | solution.py:95
  22.9 43.2 %while.11 = (s32[]{:T(128)}, f32[6,8192]{1,0:T(8,128)S(1)}, f32[8,6,512]{2,1,0:T(8,128)S(1)}, s32[8,512]{1,0:T(8,128)S(1)}, s32[]{:T(128)}, /*index=5*/s32[]{:T(128)}) while((s32[]{:T(128)}, f32[6,8192]{1,0:T(8,128)S(1)}, f32[8,6,512]{2,1,0:T(8,128)S(1)}, s32[8,512]{1,0:T(8,128)S(1)}, s32[]{:T(128)}, /*index=5*/s32[]{:T(128)}) %tuple.39), condition=%wide.region_2.3_spmd.clone, body=%wide.region_1.2_spmd.clone.sunk | while | flops 306282496 | bytes 481367 | solution.py:122
  23.0 5.4 %fusion.58 = f32[6,8192]{1,0:T(8,128)S(1)} fusion(s32[512]{0:T(512)S(1)} %bitcast.121, f32[6,8192]{1,0:T(8,128)S(1)} %get-tuple-element.113, pred[]{:T(512)S(6)} %compare.15, f32[8,6,512]{2,1,0:T(8,128)S(1)} %get-tuple-element.120, s32[]{:T(128)} %get-tuple-element.112), kind=kOutput, calls=%fused_computation.3.clone.1 | convolution fusion | flops 306282496 | bytes 477189 | tf_op jit(solution)/shard_map/while/body/eval_jaxpr/dot_general | solution.py:118
  28.4 5.4 %fusion.58 = f32[6,8192]{1,0:T(8,128)S(1)} fusion(s32[512]{0:T(512)S(1)} %bitcast.121, f32[6,8192]{1,0:T(8,128)S(1)} %get-tuple-element.113, pred[]{:T(512)S(6)} %compare.15, f32[8,6,512]{2,1,0:T(8,128)S(1)} %get-tuple-element.120, s32[]{:T(128)} %get-tuple-element.112), kind=kOutput, calls=%fused_computation.3.clone.1 | convolution fusion | flops 306282496 | bytes 477189 | tf_op jit(solution)/shard_map/while/body/eval_jaxpr/dot_general | solution.py:118
  33.8 5.4 %fusion.58 = f32[6,8192]{1,0:T(8,128)S(1)} fusion(s32[512]{0:T(512)S(1)} %bitcast.121, f32[6,8192]{1,0:T(8,128)S(1)} %get-tuple-element.113, pred[]{:T(512)S(6)} %compare.15, f32[8,6,512]{2,1,0:T(8,128)S(1)} %get-tuple-element.120, s32[]{:T(128)} %get-tuple-element.112), kind=kOutput, calls=%fused_computation.3.clone.1 | convolution fusion | flops 306282496 | bytes 477189 | tf_op jit(solution)/shard_map/while/body/eval_jaxpr/dot_general | solution.py:118
  39.1 5.4 %fusion.58 = f32[6,8192]{1,0:T(8,128)S(1)} fusion(s32[512]{0:T(512)S(1)} %bitcast.121, f32[6,8192]{1,0:T(8,128)S(1)} %get-tuple-element.113, pred[]{:T(512)S(6)} %compare.15, f32[8,6,512]{2,1,0:T(8,128)S(1)} %get-tuple-element.120, s32[]{:T(128)} %get-tuple-element.112), kind=kOutput, calls=%fused_computation.3.clone.1 | convolution fusion | flops 306282496 | bytes 477189 | tf_op jit(solution)/shard_map/while/body/eval_jaxpr/dot_general | solution.py:118
  44.5 5.4 %fusion.58 = f32[6,8192]{1,0:T(8,128)S(1)} fusion(s32[512]{0:T(512)S(1)} %bitcast.121, f32[6,8192]{1,0:T(8,128)S(1)} %get-tuple-element.113, pred[]{:T(512)S(6)} %compare.15, f32[8,6,512]{2,1,0:T(8,128)S(1)} %get-tuple-element.120, s32[]{:T(128)} %get-tuple-element.112), kind=kOutput, calls=%fused_computation.3.clone.1 | convolution fusion | flops 306282496 | bytes 477189 | tf_op jit(solution)/shard_map/while/body/eval_jaxpr/dot_general | solution.py:118
  49.9 5.4 %fusion.58 = f32[6,8192]{1,0:T(8,128)S(1)} fusion(s32[512]{0:T(512)S(1)} %bitcast.121, f32[6,8192]{1,0:T(8,128)S(1)} %get-tuple-element.113, pred[]{:T(512)S(6)} %compare.15, f32[8,6,512]{2,1,0:T(8,128)S(1)} %get-tuple-element.120, s32[]{:T(128)} %get-tuple-element.112), kind=kOutput, calls=%fused_computation.3.clone.1 | convolution fusion | flops 306282496 | bytes 477189 | tf_op jit(solution)/shard_map/while/body/eval_jaxpr/dot_general | solution.py:118
  55.3 5.4 %fusion.58 = f32[6,8192]{1,0:T(8,128)S(1)} fusion(s32[512]{0:T(512)S(1)} %bitcast.121, f32[6,8192]{1,0:T(8,128)S(1)} %get-tuple-element.113, pred[]{:T(512)S(6)} %compare.15, f32[8,6,512]{2,1,0:T(8,128)S(1)} %get-tuple-element.120, s32[]{:T(128)} %get-tuple-element.112), kind=kOutput, calls=%fused_computation.3.clone.1 | convolution fusion | flops 306282496 | bytes 477189 | tf_op jit(solution)/shard_map/while/body/eval_jaxpr/dot_general | solution.py:118
  60.7 5.4 %fusion.58 = f32[6,8192]{1,0:T(8,128)S(1)} fusion(s32[512]{0:T(512)S(1)} %bitcast.121, f32[6,8192]{1,0:T(8,128)S(1)} %get-tuple-element.113, pred[]{:T(512)S(6)} %compare.15, f32[8,6,512]{2,1,0:T(8,128)S(1)} %get-tuple-element.120, s32[]{:T(128)} %get-tuple-element.112), kind=kOutput, calls=%fused_computation.3.clone.1 | convolution fusion | flops 306282496 | bytes 477189 | tf_op jit(solution)/shard_map/while/body/eval_jaxpr/dot_general | solution.py:118
  67.4 11.5 %all-to-all-start.2 = ((f32[128,1,384]{2,1,0:T(1,128)}), f32[128,1,384]{2,1,0:T(1,128)S(1)}, u32[]{:S(2)}, u32[]{:S(2)}) async-start(f32[128,1,384]{2,1,0:T(1,128)} %reshape.156), calls=%async_computation.2 | async-start | bytes 393216 | tf_op jit(solution)/shard_map/all_to_all | solution.py:126
  80.7 8.4 %all-to-all-done.2 = f32[128,1,384]{2,1,0:T(1,128)S(1)} async-done(((f32[128,1,384]{2,1,0:T(1,128)}), f32[128,1,384]{2,1,0:T(1,128)S(1)}, u32[]{:S(2)}, u32[]{:S(2)}) %all-to-all-start.2) | async-done | bytes 196640 | tf_op jit(solution)/shard_map/all_to_all | solution.py:126
  89.1 4.3 all-to-all-start
  97.5 30.3 %all-to-all-done = f32[5,32,16,256]{3,2,0,1:T(8,128)S(1)} async-done(((f32[5,32,16,256]{3,2,0,1:T(8,128)}), f32[5,32,16,256]{3,2,0,1:T(8,128)S(1)}, u32[]{:S(2)}, u32[]{:S(2)}) %all-to-all-start) | async-done | bytes 2621472 | tf_op jit(solution)/shard_map/all_to_all | solution.py:74
  129.4 29.2 %copy.44 = f32[5,1,16,8192]{2,1,0,3:T(1,128)} copy(f32[5,1,16,8192]{3,2,0,1:T(8,128)S(1)} %fusion.34) | data formatting | bytes 5242880 | tf_op jit(solution)/shard_map/dynamic_slice | solution.py:80
  158.6 66.6 %reduce.16 = f32[8192,5,16]{2,1,0:T(8,128)} reduce(f32[8192,5,1,16]{3,2,1,0:T(1,128)} %bitcast.99, f32[]{:T(128)} %broadcast.138), dimensions={2}, to_apply=%bitcast.88.reduce_sub_computation | reduce | bytes 5242884
  225.2 20.8 %reshape.154 = f32[32,1,20480]{2,1,0:T(1,128)} reshape(f32[8192,5,16]{2,1,0:T(8,128)} %reduce.16) | data formatting | bytes 5242880
  246.0 6.5 %all-to-all-start.1 = ((f32[32,1,20480]{2,1,0:T(1,128)}), f32[32,1,20480]{2,1,0:T(1,128)S(1)}, u32[]{:S(2)}, u32[]{:S(2)}) async-start(f32[32,1,20480]{2,1,0:T(1,128)} %reshape.154), calls=%async_computation.1 | async-start | bytes 5242880 | tf_op jit(solution)/shard_map/all_to_all | solution.py:87
  254.0 4.3 fusion.20
  258.3 28.1 %all-to-all-done.1 = f32[32,1,20480]{2,1,0:T(1,128)S(1)} async-done(((f32[32,1,20480]{2,1,0:T(1,128)}), f32[32,1,20480]{2,1,0:T(1,128)S(1)}, u32[]{:S(2)}, u32[]{:S(2)}) %all-to-all-start.1) | async-done | bytes 2621472 | tf_op jit(solution)/shard_map/all_to_all | solution.py:87
  286.4 9.2 %reduce.17 = f32[32,20480]{1,0:T(8,128)} reduce(f32[32,1,20480]{2,1,0:T(1,128)S(1)} %all-to-all-done.1, f32[]{:T(128)} %broadcast.138), dimensions={1}, to_apply=%all_to_all.31.reduce_sub_computation | reduce | bytes 5242884 | tf_op jit(solution)/shard_map/all_to_all | solution.py:87
  295.6 55.7 %reshape.155 = f32[8192,5,1,16]{3,2,1,0:T(1,128)} reshape(f32[32,20480]{1,0:T(8,128)} %reduce.17) | data formatting | bytes 5242880
  351.3 38.4 %copy.45 = f32[5,1,16,8192]{3,2,0,1:T(8,128)} copy(f32[5,1,16,8192]{2,1,0,3:T(1,128)} %bitcast.100) | data formatting | bytes 5242880 | tf_op jit(solution)/shard_map/all_to_all | solution.py:87
  395.8 3.0 copy.51
  398.9 31.0 %multiply_reduce_fusion = f32[8192,3]{0,1:T(4,128)S(1)} fusion(f32[8192,256]{0,1:T(8,128)} %fusion.20, f32[512,3,256]{0,2,1:T(8,128)} %copy.51, s32[8192]{0:T(1024)S(1)} %get-tuple-element.79), kind=kOutput, calls=%fused_computation.14 | convolution fusion | flops 38671458304 | bytes 10092544 | tf_op jit(solution)/shard_map/dot_general | solution.py:142
  430.6 26.3 %fusion.9 = f32[512,3,256]{2,0,1:T(8,128)} fusion(f32[8192,3]{0,1:T(4,128)S(1)} %get-tuple-element.78, f32[8192,256]{0,1:T(8,128)} %fusion.20, s32[8192]{0:T(1024)S(1)} %get-tuple-element.79), kind=kOutput, calls=%fused_computation.11 | convolution fusion | flops 38665191424 | bytes 10092544 | tf_op jit(solution)/shard_map/dot_general | solution.py:152
  456.9 3.6 constant_dynamic-update-slice_fusion.1
  465.5 4.5 fusion.54
  475.2 5.7 %collective-permute-start.3 = (f32[7,32,16,2]{1,2,3,0:T(8,128)}, f32[7,32,16,2]{1,2,3,0:T(8,128)}, u32[]{:S(2)}, u32[]{:S(2)}) collective-permute-start(f32[7,32,16,2]{1,2,3,0:T(8,128)} %copy.56), channel_id=1, source_target_pairs={{1,0},{2,1},{3,2},{4,3},{5,4},{6,5},{7,6},{8,7},{9,8},{10,9},{11,1... | collective-permute-start | bytes 86024 | tf_op jit(solution)/shard_map/ppermute | solution.py:28
  481.7 6.0 %collective-permute-start = (f32[7,2,16,256]{3,1,2,0:T(2,128)}, f32[7,2,16,256]{3,1,2,0:T(2,128)S(1)}, u32[]{:S(2)}, u32[]{:S(2)}) collective-permute-start(f32[7,2,16,256]{3,1,2,0:T(2,128)} %get-tuple-element.71), channel_id=1, source_target_pairs={{0,32},{32,64},{64,96},{1,33},{33,65},{65,97},{2,34},{34,66},{66,9... | collective-permute-start | bytes 688136 | tf_op jit(solution)/shard_map/ppermute | solution.py:26
  497.2 3.8 minimum_multiply_fusion
  504.0 3.1 minimum_multiply_fusion.1
  (87 shorter events, 47.8 us)
Async XLA Ops:
  2.1 20.7 %copy-start.6 = (f32[3,4096]{1,0:T(4,128)S(1)}, f32[3,4096]{1,0:T(4,128)}, u32[]{:S(2)}) copy-start(f32[3,4096]{1,0:T(4,128)} %param.11) | copy-start | bytes 147460
  2.1 20.7 %copy-start.7 = (f32[4096]{0:T(1024)S(1)}, f32[4096]{0:T(1024)}, u32[]{:S(2)}) copy-start(f32[4096]{0:T(1024)} %param.13) | copy-start | bytes 49156
  2.2 20.7 %copy-start.8 = (f32[4096]{0:T(1024)S(1)}, f32[4096]{0:T(1024)}, u32[]{:S(2)}) copy-start(f32[4096]{0:T(1024)} %param.12) | copy-start | bytes 49156
  66.1 12.8 %copy-start.4 = (f32[5,32,16,256]{3,2,1,0:T(8,128)S(1)}, f32[5,32,16,256]{3,2,1,0:T(8,128)}, u32[]{:S(2)}) copy-start(f32[5,32,16,256]{3,2,1,0:T(8,128)} %param.9) | copy-start | bytes 7864324
  67.4 21.7 %all-to-all-start.2 = ((f32[128,1,384]{2,1,0:T(1,128)}), f32[128,1,384]{2,1,0:T(1,128)S(1)}, u32[]{:S(2)}, u32[]{:S(2)}) async-start(f32[128,1,384]{2,1,0:T(1,128)} %reshape.156), calls=%async_computation.2 | async-start | bytes 393216 | tf_op jit(solution)/shard_map/all_to_all | solution.py:126
  80.7 12.7 %copy-start.9 = (s32[32]{0:T(128)S(1)}, s32[32]{0:T(128)}, u32[]{:S(2)}) copy-start(s32[32]{0:T(128)} %param.10) | copy-start | bytes 388
  89.1 38.6 %all-to-all-start = ((f32[5,32,16,256]{3,2,0,1:T(8,128)}), f32[5,32,16,256]{3,2,0,1:T(8,128)S(1)}, u32[]{:S(2)}, u32[]{:S(2)}) async-start(f32[5,32,16,256]{3,2,0,1:T(8,128)} %copy.42), calls=%async_computation | async-start | bytes 5242880 | tf_op jit(solution)/shard_map/all_to_all | solution.py:74
  246.0 40.4 %all-to-all-start.1 = ((f32[32,1,20480]{2,1,0:T(1,128)}), f32[32,1,20480]{2,1,0:T(1,128)S(1)}, u32[]{:S(2)}, u32[]{:S(2)}) async-start(f32[32,1,20480]{2,1,0:T(1,128)} %reshape.154), calls=%async_computation.1 | async-start | bytes 5242880 | tf_op jit(solution)/shard_map/all_to_all | solution.py:87
  460.5 1.8 copy-start.2
  472.3 17.4 %collective-permute-start.2 = (f32[7,32,16,2]{1,2,3,0:T(8,128)S(1)}, f32[7,32,16,2]{1,2,3,0:T(8,128)}, u32[]{:S(2)}, u32[]{:S(2)}) collective-permute-start(f32[7,32,16,2]{1,2,3,0:T(8,128)S(1)} %copy.54), channel_id=1, source_target_pairs={{0,1},{1,2},{2,3},{3,4},{4,5},{5,6},{6,7},{7,8},{8,9},{9,10},{10,1... | collective-permute-start | bytes 86024 | tf_op jit(solution)/shard_map/ppermute | solution.py:26
  475.2 16.1 %collective-permute-start.3 = (f32[7,32,16,2]{1,2,3,0:T(8,128)}, f32[7,32,16,2]{1,2,3,0:T(8,128)}, u32[]{:S(2)}, u32[]{:S(2)}) collective-permute-start(f32[7,32,16,2]{1,2,3,0:T(8,128)} %copy.56), channel_id=1, source_target_pairs={{1,0},{2,1},{3,2},{4,3},{5,4},{6,5},{7,6},{8,7},{9,8},{10,9},{11,1... | collective-permute-start | bytes 86024 | tf_op jit(solution)/shard_map/ppermute | solution.py:28
  481.7 22.0 %collective-permute-start = (f32[7,2,16,256]{3,1,2,0:T(2,128)}, f32[7,2,16,256]{3,1,2,0:T(2,128)S(1)}, u32[]{:S(2)}, u32[]{:S(2)}) collective-permute-start(f32[7,2,16,256]{3,1,2,0:T(2,128)} %get-tuple-element.71), channel_id=1, source_target_pairs={{0,32},{32,64},{64,96},{1,33},{33,65},{65,97},{2,34},{34,66},{66,9... | collective-permute-start | bytes 688136 | tf_op jit(solution)/shard_map/ppermute | solution.py:26
  487.7 16.1 %collective-permute-start.1 = (f32[7,2,16,256]{3,1,2,0:T(2,128)S(1)}, f32[7,2,16,256]{3,1,2,0:T(2,128)S(1)}, u32[]{:S(2)}, u32[]{:S(2)}) collective-permute-start(f32[7,2,16,256]{3,1,2,0:T(2,128)S(1)} %get-tuple-element.72), channel_id=1, source_target_pairs={{32,0},{64,32},{96,64},{33,1},{65,33},{97,65},{34,2},{66,34},{98,6... | collective-permute-start | bytes 688136 | tf_op jit(solution)/shard_map/ppermute | solution.py:28
  494.2 2.4 copy-start
  494.2 3.0 copy-start.1
  507.2 1.9 copy-start.3
  507.2 1.9 copy-start.5
